TPU v7x, 32 devices: a whole 2x2x4 slice. The times are simulated.
32 devices in a mesh: grp: 4 (over z), emb: 8 (over y, x, core).
Axes of the slice: x: 2, y: 2, z: 4, core: 2. Of those that a mesh axis runs over, the one named last changes fastest.
Arguments:
- bottom_out: bfloat16 [4096, 128], P(('grp', 'emb')), may hold values from -6 to 6
- owner_ids: int32 [106496, 1], P(('grp', 'emb')), may hold values from 0 to 7; in each aligned block of 3328 rows (0 to 3327, 3328 to 6655, ...) at most 624 rows name the same one
- row_ids: int32 [4096, 26], P(('grp', 'emb')), may hold values from 0 to 95
- positions: int32 [4096], P(('grp', 'emb')), may hold values from 0 to 15
- labels: int32 [4096], P(('grp', 'emb')), may hold values 0 or 1
- tables: bfloat16 [26, 768, 128], P(None, 'emb'), may hold values from -6 to 6
- cross_down: bfloat16 [3456, 512], replicated, may hold values from -0.109375 to 0.109375
- cross_up: bfloat16 [512, 3456], replicated, may hold values from -0.25 to 0.25
- cross_bias: float32 [3456], replicated, may hold values from -3 to 3
- out_weight: bfloat16 [3456], replicated, may hold values from -0.109375 to 0.109375
- position_bias: float32 [16], replicated, may hold values from -2 to 2
Outputs:
- table_grad: float32 [26, 768, 128], P(None, 'emb')
- bottom_grad: bfloat16 [4096, 128], P(('grp', 'emb'))
- bias_grad: float32 [3456], replicated
Inputs may be any that keep to these rules, and one draw needn't show every extreme that they name: `owner_ids`: in every aligned block of 3328 lookups (the lookups of one device) no owner is named more than 624 times, and in some block one owner is named exactly 624 times.
All inputs are finite; a program needn't handle non-finite values. No bound on the sum of `labels` on one device may be relied on, other than what follows from the above.
Results may differ from a plain program's by a relative error of at most 0.0085.
Values may be sent and summed in bfloat16 or wider, within the bound.
No kernel may reach another device: no remote copies, remote signals or barrier semaphores. Data moves between devices by JAX's collectives and lax.ppermute only.
A program may use at most 64 MiB of HBM per device.

v0:
```python
import jax
import jax.numpy as jnp
from jax import lax
from jax.sharding import PartitionSpec as P


def local(
    bottom_out,
    owner_ids,
    row_ids,
    positions,
    labels,
    tables,
    cross_down,
    cross_up,
    cross_bias,
    out_weight,
    position_bias,
):
    sample_count, table_count = row_ids.shape
    rows_local = tables.shape[1]
    row_width = tables.shape[2]
    owner_count = lax.axis_size("emb")
    capacity = 3 * sample_count * table_count // (2 * owner_count)
    lookup_count = sample_count * table_count
    owners = owner_ids.reshape(sample_count, table_count)
    flat_owner = owners.reshape(-1)
    local_grid = jnp.arange(table_count, dtype=jnp.int32)[None, :] * rows_local + row_ids
    local_index = local_grid.reshape(-1)
    owner_marks = (flat_owner[:, None] == jnp.arange(owner_count, dtype=jnp.int32)[None, :]).astype(
        jnp.int32
    )
    ranking = jnp.cumsum(owner_marks, axis=0) - 1
    slot_index = jnp.sum(ranking * owner_marks, axis=1)
    buffer_place = flat_owner * capacity + slot_index
    flat_table = tables.reshape(table_count * rows_local, row_width)
    request = jnp.zeros((owner_count * capacity,), jnp.int32).at[buffer_place].set(local_index)
    request = request.reshape(owner_count, capacity)
    received = lax.all_to_all(request, "emb", split_axis=0, concat_axis=0, tiled=True)
    fetched = flat_table[received]
    arrived = lax.all_to_all(fetched, "emb", split_axis=0, concat_axis=0, tiled=True)
    pooled = arrived.reshape(owner_count * capacity, row_width)[buffer_place].reshape(
        sample_count, table_count * row_width
    )
    first = jnp.concatenate([bottom_out, pooled], axis=1)
    first_wide = first.astype(jnp.float32)
    weight_row = out_weight.astype(jnp.float32)
    reduced = jnp.dot(first, cross_down, preferred_element_type=jnp.float32).astype(jnp.bfloat16)
    gate_scale = jnp.dot(reduced, cross_up, preferred_element_type=jnp.float32) + cross_bias
    crossed = first_wide * gate_scale + first_wide
    position_marks = (
        positions[:, None] == jnp.arange(position_bias.shape[0], dtype=jnp.int32)[None, :]
    ).astype(jnp.float32)
    logit = jnp.sum(crossed * weight_row[None, :], axis=1) + jnp.sum(
        position_marks * position_bias[None, :], axis=1
    )
    err = jax.nn.sigmoid(logit) - labels.astype(jnp.float32)
    cotangent = err[:, None] * weight_row[None, :]
    scaled = cotangent * first_wide
    down_grad = lax.dot_general(
        scaled.astype(jnp.bfloat16),
        cross_up,
        (((1,), (1,)), ((), ())),
        preferred_element_type=jnp.float32,
    ).astype(jnp.bfloat16)
    back_term = lax.dot_general(
        down_grad, cross_down, (((1,), (1,)), ((), ())), preferred_element_type=jnp.float32
    )
    input_grad = (cotangent * (gate_scale + 1.0) + back_term).astype(jnp.bfloat16)
    bottom_grad = input_grad[:, :row_width]
    row_grads = input_grad[:, row_width:].reshape(lookup_count, row_width)
    outgoing = (
        jnp.zeros((owner_count * capacity, row_width), jnp.bfloat16).at[buffer_place].set(row_grads)
    )
    incoming = lax.all_to_all(
        outgoing.reshape(owner_count, capacity, row_width),
        "emb",
        split_axis=0,
        concat_axis=0,
        tiled=True,
    )
    local_grad = (
        jnp.zeros((table_count * rows_local, row_width), jnp.float32)
        .at[received.reshape(-1)]
        .add(incoming.reshape(owner_count * capacity, row_width).astype(jnp.float32))
    )
    summed_grad = lax.psum(local_grad.astype(jnp.bfloat16), "grp").astype(jnp.float32)
    table_grad = summed_grad.reshape(table_count, rows_local, row_width)
    bias_local = jnp.sum(scaled, axis=0)
    bias_grad = lax.psum(bias_local, ("grp", "emb"))
    return (table_grad, bottom_grad, bias_grad)


def solution(mesh):
    placed = (
        P(("grp", "emb"), None),
        P(("grp", "emb"), None),
        P(("grp", "emb"), None),
        P(("grp", "emb")),
        P(("grp", "emb")),
        P(None, "emb", None),
        P(),
        P(),
        P(),
        P(),
        P(),
    )
    return jax.shard_map(
        local,
        mesh=mesh,
        in_specs=placed,
        out_specs=(P(None, "emb", None), P(("grp", "emb"), None), P()),
        check_vma=False,
    )
```

profile of v0, /device:TPU:0, one launch (start us, length us, event | category | flops | bytes accessed | tf_op | source)
XLA Modules:
  0.0 242.6 jit_solution(920060485825970964)
XLA Ops:
  7.2 0.0 copy-start
  7.2 0.9 broadcast_add_fusion
  8.1 0.7 copy.15
  8.9 1.6 reshape.157
  10.4 0.7 reduce
  11.2 0.7 fusion.17
  11.9 5.2 %reduce-window.6 = s32[8,26,128]{2,1,0:T(8,128)} reduce-window(s32[8,26,128]{2,1,0:T(8,128)} %fusion.17, s32[]{:T(128)} %constant.10.clone.1), window={size=1x1x128 pad=0_0x0_0x127_0}, to_apply=%region_0.0 | reduce-window | flops 3381248 | bytes 212996 | tf_op jit(solution)/shard_map/reduce-window
  17.1 1.8 slice_reduce_fusion
  18.9 1.5 reduce-window.9
  20.3 1.0 add_bitcast_fusion
  21.4 0.1 fusion.19
  21.5 0.8 fusion.22
  22.2 0.0 copy-start.2
  22.2 13.5 %scatter_custom_fusion = s32[4992]{0:T(1024)} fusion(s32[3328]{0:T(1024)S(1)} %fusion.22, s32[3328]{0:T(1024)} %reshape.157, s32[]{:T(128)} %constant.10.clone.1), kind=kCustom, calls=%fused_computation.40 | custom fusion | bytes 20480 | tf_op jit(solution)/shard_map/scatter | solution.py:37
  35.7 1.4 all_to_all.14
  37.1 9.9 %all_to_all.22 = s32[8,1,624]{2,1,0:T(1,128)S(1)} all-to-all(s32[8,1,624]{2,1,0:T(1,128)} %all_to_all.14), channel_id=1, replica_groups=mesh['grp'=4,'emb'=8] {'emb'}, dimensions={0} | all-to-all | bytes 39936 | tf_op jit(solution)/shard_map/all_to_all | solution.py:39
  47.1 0.0 copy-start.1
  47.1 0.6 copy-done.1
  47.7 0.7 fusion.20
  48.3 1.4 reshape.139
  49.8 1.3 pad_clamp_fusion
  51.1 12.3 %gather_fusion = bf16[4992,128]{1,0:T(8,128)(2,1)} fusion(bf16[2496,128]{1,0:T(8,128)(2,1)} %bitcast.32, s32[5120]{0:T(1024)} %pad_clamp_fusion), kind=kCustom, calls=%fused_computation | custom fusion | bytes 2575872 | tf_op jit(solution)/shard_map/gather | solution.py:40
  63.4 0.0 copy-done.2
  63.4 4.3 %all-to-all-start.1 = ((bf16[8,624,128]{2,1,0:T(8,128)(2,1)}), bf16[8,624,128]{2,1,0:T(8,128)(2,1)}, u32[]{:S(2)}, u32[]{:S(2)}) async-start(bf16[8,624,128]{2,1,0:T(8,128)(2,1)} %bitcast.34), calls=%async_computation.1 | async-start | bytes 2555904 | tf_op jit(solution)/shard_map/all_to_all | solution.py:41
  67.6 0.7 convert_element_type.40
  68.3 1.3 pad_clamp_fusion.1
  69.7 1.4 constant_dynamic-update-slice_fusion.1
  71.0 1.2 select_reduce_fusion
  72.3 13.2 %all-to-all-done.1 = bf16[8,624,128]{2,1,0:T(8,128)(2,1)} async-done(((bf16[8,624,128]{2,1,0:T(8,128)(2,1)}), bf16[8,624,128]{2,1,0:T(8,128)(2,1)}, u32[]{:S(2)}, u32[]{:S(2)}) %all-to-all-start.1) | async-done | bytes 1277984 | tf_op jit(solution)/shard_map/all_to_all | solution.py:41
  85.5 9.2 %gather_fusion.1 = bf16[3328,128]{1,0:T(8,128)(2,1)} fusion(bf16[4992,128]{1,0:T(8,128)(2,1)} %bitcast.4, s32[4096]{0:T(1024)} %pad_clamp_fusion.1), kind=kCustom, calls=%fused_computation.1 | custom fusion | bytes 1717248 | tf_op jit(solution)/shard_map/gather | solution.py:42
  94.7 2.8 %reshape.131 = bf16[128,3328]{1,0:T(8,128)(2,1)} reshape(bf16[3328,128]{1,0:T(8,128)(2,1)} %gather_fusion.1) | data formatting | bytes 1703936 | tf_op jit(solution)/shard_map/reshape | solution.py:42
  97.5 2.1 constant_dynamic-update-slice_fusion
  99.6 0.0 copy-done
  99.6 5.6 %fusion.6 = (f32[128]{0:T(128)}, f32[128,3456]{1,0:T(8,128)}) fusion(bf16[128,3456]{1,0:T(8,128)(2,1)} %constant_dynamic-update-slice_fusion, f32[3456]{0:T(1024)S(1)} %convert_element_type.40, f32[3456]{0:T(1024)} %param.19, bf16[512,3456]{1,0:T(8,128)(2,1)} %param.18, bf16[3456,512]{1,0:T(8,128)(2,1)S(1)} %copy-done), kind=kOutput, calls=%fused_computation.16 | convolution fusion | flops 908689280 | bytes 9760256 | tf_op jit(solution)/shard_map/dot_general | solution.py:49
  105.2 1.2 divide_subtract_fusion
  106.4 6.1 %fusion = bf16[128,3456]{1,0:T(8,128)(2,1)} fusion(bf16[3456,512]{1,0:T(8,128)(2,1)S(1)} %copy-done, f32[128,3456]{1,0:T(8,128)} %get-tuple-element.4, bf16[512,3456]{1,0:T(8,128)(2,1)} %param.18, bf16[128,3456]{1,0:T(8,128)(2,1)} %constant_dynamic-update-slice_fusion, f32[128]{0:T(128)} %divide_subtract_fusion, f32[3456]{0:T(1024)S(1)} %convert_element_type.40), kind=kOutput, calls=%fused_computation.7 | convolution fusion | flops 910016512 | bytes 10631168 | tf_op jit(solution)/shard_map/dot_general | solution.py:66
  112.4 2.1 slice.21
  114.5 2.9 %reshape.165 = bf16[3328,128]{1,0:T(8,128)(2,1)} reshape(bf16[128,3328]{1,0:T(8,128)(2,1)} %slice.21) | data formatting | bytes 1703936 | tf_op jit(solution)/shard_map/reshape | solution.py:71
  117.4 14.9 %scatter_custom_fusion.1 = bf16[4992,128]{1,0:T(8,128)(2,1)} fusion(s32[3328]{0:T(1024)} %copy-done.2, bf16[3328,128]{1,0:T(8,128)(2,1)} %reshape.165, bf16[]{:T(256)} %constant.5.clone.1), kind=kCustom, calls=%fused_computation.21 | custom fusion | bytes 1278464 | tf_op jit(solution)/shard_map/scatter | solution.py:73
  132.3 4.3 %all-to-all-start.2 = ((bf16[8,624,128]{2,1,0:T(8,128)(2,1)}), bf16[8,624,128]{2,1,0:T(8,128)(2,1)}, u32[]{:S(2)}, u32[]{:S(2)}) async-start(bf16[8,624,128]{2,1,0:T(8,128)(2,1)} %bitcast.33), calls=%async_computation.2 | async-start | bytes 2555904 | tf_op jit(solution)/shard_map/all_to_all | solution.py:75
  136.5 0.2 all-reduce.2.cloned.1.call-start
  136.8 1.4 reduce.4
  138.2 1.4 reshape.128
  139.6 1.4 fusion.21
  141.0 13.4 %all-to-all-done.2 = bf16[8,624,128]{2,1,0:T(8,128)(2,1)} async-done(((bf16[8,624,128]{2,1,0:T(8,128)(2,1)}), bf16[8,624,128]{2,1,0:T(8,128)(2,1)}, u32[]{:S(2)}, u32[]{:S(2)}) %all-to-all-start.2) | async-done | bytes 1277984 | tf_op jit(solution)/shard_map/all_to_all | solution.py:75
  154.4 33.9 %scatter_custom_fusion.2 = f32[2496,128]{1,0:T(8,128)} fusion(s32[4992]{0:T(1024)} %fusion.21, bf16[4992,128]{1,0:T(8,128)(2,1)} %bitcast.8, f32[]{:T(128)} %constant.9.clone.1), kind=kCustom, calls=%fused_computation.9 | custom fusion | flops 1277952 | bytes 2556416 | tf_op jit(solution)/shard_map/scatter-add | solution.py:85
  188.4 2.2 convert_element_type.47
  190.6 0.0 all-reduce.2.cloned.1.call-update
  190.6 1.4 slice.22
  192.0 2.1 fusion.3
  194.1 39.5 %psum.15 = f32[3456]{0:T(1024)} all-reduce(f32[3456]{0:T(1024)} %fusion.3), channel_id=1, replica_groups=mesh['grp'=4,'emb'=8] {'grp','emb'}, use_global_device_ids=true, to_apply=%region_10.11 | all-reduce | flops 3456 | bytes 27648 | tf_op jit(solution)/shard_map/psum | solution.py:90
  233.5 0.0 all-reduce.2.cloned.1.call-done
  233.5 2.3 reshape.135
  (1 shorter events, 0.0 us)
Async XLA Ops:
  7.2 92.5 %copy-start = (bf16[3456,512]{1,0:T(8,128)(2,1)S(1)}, bf16[3456,512]{1,0:T(8,128)(2,1)}, u32[]{:S(2)}) copy-start(bf16[3456,512]{1,0:T(8,128)(2,1)} %param.17) | copy-start | bytes 10616836
  22.2 41.2 %copy-start.2 = (s32[3328]{0:T(1024)}, s32[3328]{0:T(1024)S(1)}, u32[]{:S(2)}) copy-start(s32[3328]{0:T(1024)S(1)} %fusion.22) | copy-start | bytes 39940
  47.1 0.6 copy-start.1
  63.4 22.1 %all-to-all-start.1 = ((bf16[8,624,128]{2,1,0:T(8,128)(2,1)}), bf16[8,624,128]{2,1,0:T(8,128)(2,1)}, u32[]{:S(2)}, u32[]{:S(2)}) async-start(bf16[8,624,128]{2,1,0:T(8,128)(2,1)} %bitcast.34), calls=%async_computation.1 | async-start | bytes 2555904 | tf_op jit(solution)/shard_map/all_to_all | solution.py:41
  132.3 22.1 %all-to-all-start.2 = ((bf16[8,624,128]{2,1,0:T(8,128)(2,1)}), bf16[8,624,128]{2,1,0:T(8,128)(2,1)}, u32[]{:S(2)}, u32[]{:S(2)}) async-start(bf16[8,624,128]{2,1,0:T(8,128)(2,1)} %bitcast.33), calls=%async_computation.2 | async-start | bytes 2555904 | tf_op jit(solution)/shard_map/all_to_all | solution.py:75
  136.5 97.0 %all-reduce.2.cloned.1.call-start = ((), (), s32[]{:S(2)}) async-start(), calls=%async_computation.3 | async-start | bytes 1277952 | tf_op jit(solution)/shard_map/psum | solution.py:87
Sparse Core Ops, SparseCore 0:
  190.7 39.9 all-reduce.1
where the time goes:
time: 245 us; the launch traced here: 243 us
  local copies, waits for them, and re-layouts  71.5 us (29%)
  other arithmetic  60.6 us (25%)
  blocking collectives  49.4 us (20%)
  waiting for transfers between devices  26.7 us (11%)
  between operations  14.1 us (6%)
  matrix products  11.6 us (5%)
  starting transfers between devices  8.73 us (4%)
    psum x1, blocking collectives, local(): bias_grad = lax.psum(bias_local, ('grp', 'emb'))  39.5 us
    scatter-add x1, other arithmetic, local(): local_grad = jnp.zeros((table_count * rows_local, row_width), jnp.float32...  33.9 us
    scatter x1, local copies, waits for them, and re-layouts, local(): jnp.zeros((owner_count * capacity, row_width), jnp.bfloat16)  14.9 us
    scatter x1, local copies, waits for them, and re-layouts, local(): jnp.zeros((owner_count * capacity,), jnp.int32).at[buffer_place]  13.5 us
    all_to_all x1, waiting for transfers between devices, local(): lax.all_to_all(outgoing.reshape(owner_count, capacity, row_width), 'emb',...  13.4 us
    all_to_all x1, waiting for transfers between devices, local(): lax.all_to_all(fetched, 'emb', split_axis=0, concat_axis=0, tiled=True)  13.2 us
    gather x1, local copies, waits for them, and re-layouts, local(): fetched = flat_table[received]  12.3 us
    all_to_all x1, blocking collectives, local(): lax.all_to_all(request, 'emb', split_axis=0, concat_axis=0, tiled=True)  9.94 us
  transfers between devices with their start and end apart: 3, of which 2 were waited for; matrix products, arithmetic and copies ran while one was open for 5% of the time, Pallas kernels for 0%

commit v1 on v0

--- a/solution.py
+++ b/solution.py
@@ -87,7 +87,7 @@
     summed_grad = lax.psum(local_grad.astype(jnp.bfloat16), "grp").astype(jnp.float32)
     table_grad = summed_grad.reshape(table_count, rows_local, row_width)
     bias_local = jnp.sum(scaled, axis=0)
-    bias_grad = lax.psum(bias_local, ("grp", "emb"))
+    bias_grad = jnp.sum(lax.all_gather(bias_local, ("grp", "emb")), axis=0)
     return (table_grad, bottom_grad, bias_grad)
 
 

time: 245 us -> 250 us (1.020)
  blocking collectives: 49.4 us -> 53.2 us
    all_gather x0 -> x1, blocking collectives: none -> 43.2 us  [local(): bias_grad = jnp.sum(lax.all_gather(bias_local, ('grp', 'emb')), axis=0)]
    psum x1 -> x0, blocking collectives: 39.5 us -> none  [local(): bias_grad = lax.psum(bias_local, ('grp', 'emb'))]
  transfers between devices with their start and end apart: 3 -> 3, of which waited for: 2 -> 2; matrix products, arithmetic and copies ran while one was open for 5% -> 6% of each run, Pallas kernels for 0% -> 0%
where the time goes in v1:
time: 250 us; the launch traced here: 248 us
  local copies, waits for them, and re-layouts  71.5 us (29%)
  other arithmetic  62 us (25%)
  blocking collectives  53.2 us (21%)
  waiting for transfers between devices  26.6 us (11%)
  between operations  14.1 us (6%)
  matrix products  11.6 us (5%)
  starting transfers between devices  8.73 us (3%)
    all_gather x1, blocking collectives, local(): bias_grad = jnp.sum(lax.all_gather(bias_local, ('grp', 'emb')), axis=0)  43.2 us
    scatter-add x1, other arithmetic, local(): local_grad = jnp.zeros((table_count * rows_local, row_width), jnp.float32...  33.9 us
    scatter x1, local copies, waits for them, and re-layouts, local(): jnp.zeros((owner_count * capacity, row_width), jnp.bfloat16)  14.9 us
    scatter x1, local copies, waits for them, and re-layouts, local(): jnp.zeros((owner_count * capacity,), jnp.int32).at[buffer_place]  13.5 us
    all_to_all x1, waiting for transfers between devices, local(): lax.all_to_all(outgoing.reshape(owner_count, capacity, row_width), 'emb',...  13.4 us
    all_to_all x1, waiting for transfers between devices, local(): lax.all_to_all(fetched, 'emb', split_axis=0, concat_axis=0, tiled=True)  13.2 us
    gather x1, local copies, waits for them, and re-layouts, local(): fetched = flat_table[received]  12.3 us
    all_to_all x1, blocking collectives, local(): lax.all_to_all(request, 'emb', split_axis=0, concat_axis=0, tiled=True)  9.94 us
  transfers between devices with their start and end apart: 3, of which 2 were waited for; matrix products, arithmetic and copies ran while one was open for 6% of the time, Pallas kernels for 0%

profile of v1, /device:TPU:0, one launch (start us, length us, event | category | flops | bytes accessed | tf_op | source)
XLA Modules:
  0.0 247.7 jit_solution(1146338255413169811)
XLA Ops:
  7.2 0.0 copy-start
  7.2 0.9 broadcast_add_fusion
  8.1 0.7 copy.16
  8.9 1.6 reshape.157
  10.4 0.7 reduce.1
  11.2 0.7 fusion.17
  11.9 5.2 %reduce-window.6 = s32[8,26,128]{2,1,0:T(8,128)} reduce-window(s32[8,26,128]{2,1,0:T(8,128)} %fusion.17, s32[]{:T(128)} %constant.10.clone.1), window={size=1x1x128 pad=0_0x0_0x127_0}, to_apply=%region_0.0 | reduce-window | flops 3381248 | bytes 212996 | tf_op jit(solution)/shard_map/reduce-window
  17.1 1.8 slice_reduce_fusion
  18.9 1.5 reduce-window.9
  20.3 1.0 add_bitcast_fusion
  21.4 0.1 fusion.19
  21.5 0.8 fusion.22
  22.2 0.0 copy-start.2
  22.2 13.5 %scatter_custom_fusion = s32[4992]{0:T(1024)} fusion(s32[3328]{0:T(1024)S(1)} %fusion.22, s32[3328]{0:T(1024)} %reshape.157, s32[]{:T(128)} %constant.10.clone.1), kind=kCustom, calls=%fused_computation.40 | custom fusion | bytes 20480 | tf_op jit(solution)/shard_map/scatter | solution.py:37
  35.7 1.4 all_to_all.14
  37.1 9.9 %all_to_all.22 = s32[8,1,624]{2,1,0:T(1,128)S(1)} all-to-all(s32[8,1,624]{2,1,0:T(1,128)} %all_to_all.14), channel_id=1, replica_groups=mesh['grp'=4,'emb'=8] {'emb'}, dimensions={0} | all-to-all | bytes 39936 | tf_op jit(solution)/shard_map/all_to_all | solution.py:39
  47.1 0.0 copy-start.1
  47.1 0.6 copy-done.1
  47.7 0.7 fusion.20
  48.3 1.4 reshape.139
  49.8 1.3 pad_clamp_fusion
  51.1 12.3 %gather_fusion = bf16[4992,128]{1,0:T(8,128)(2,1)} fusion(bf16[2496,128]{1,0:T(8,128)(2,1)} %bitcast.32, s32[5120]{0:T(1024)} %pad_clamp_fusion), kind=kCustom, calls=%fused_computation | custom fusion | bytes 2575872 | tf_op jit(solution)/shard_map/gather | solution.py:40
  63.4 0.0 copy-done.2
  63.4 4.3 %all-to-all-start.1 = ((bf16[8,624,128]{2,1,0:T(8,128)(2,1)}), bf16[8,624,128]{2,1,0:T(8,128)(2,1)}, u32[]{:S(2)}, u32[]{:S(2)}) async-start(bf16[8,624,128]{2,1,0:T(8,128)(2,1)} %bitcast.34), calls=%async_computation.1 | async-start | bytes 2555904 | tf_op jit(solution)/shard_map/all_to_all | solution.py:41
  67.6 0.7 convert_element_type.40
  68.3 1.3 pad_clamp_fusion.1
  69.7 1.4 constant_dynamic-update-slice_fusion.1
  71.0 1.3 select_reduce_fusion
  72.3 13.2 %all-to-all-done.1 = bf16[8,624,128]{2,1,0:T(8,128)(2,1)} async-done(((bf16[8,624,128]{2,1,0:T(8,128)(2,1)}), bf16[8,624,128]{2,1,0:T(8,128)(2,1)}, u32[]{:S(2)}, u32[]{:S(2)}) %all-to-all-start.1) | async-done | bytes 1277984 | tf_op jit(solution)/shard_map/all_to_all | solution.py:41
  85.5 9.2 %gather_fusion.1 = bf16[3328,128]{1,0:T(8,128)(2,1)} fusion(bf16[4992,128]{1,0:T(8,128)(2,1)} %bitcast.4, s32[4096]{0:T(1024)} %pad_clamp_fusion.1), kind=kCustom, calls=%fused_computation.1 | custom fusion | bytes 1717248 | tf_op jit(solution)/shard_map/gather | solution.py:42
  94.7 2.8 %reshape.131 = bf16[128,3328]{1,0:T(8,128)(2,1)} reshape(bf16[3328,128]{1,0:T(8,128)(2,1)} %gather_fusion.1) | data formatting | bytes 1703936 | tf_op jit(solution)/shard_map/reshape | solution.py:42
  97.5 2.1 constant_dynamic-update-slice_fusion
  99.6 0.0 copy-done
  99.6 5.6 %fusion.6 = (f32[128]{0:T(128)}, f32[128,3456]{1,0:T(8,128)}) fusion(bf16[128,3456]{1,0:T(8,128)(2,1)} %constant_dynamic-update-slice_fusion, f32[3456]{0:T(1024)S(1)} %convert_element_type.40, f32[3456]{0:T(1024)} %param.19, bf16[512,3456]{1,0:T(8,128)(2,1)} %param.18, bf16[3456,512]{1,0:T(8,128)(2,1)S(1)} %copy-done), kind=kOutput, calls=%fused_computation.16 | convolution fusion | flops 908689280 | bytes 9760256 | tf_op jit(solution)/shard_map/dot_general | solution.py:49
  105.2 1.2 divide_subtract_fusion
  106.4 6.1 %fusion = bf16[128,3456]{1,0:T(8,128)(2,1)} fusion(bf16[3456,512]{1,0:T(8,128)(2,1)S(1)} %copy-done, f32[128,3456]{1,0:T(8,128)} %get-tuple-element.4, bf16[512,3456]{1,0:T(8,128)(2,1)} %param.18, bf16[128,3456]{1,0:T(8,128)(2,1)} %constant_dynamic-update-slice_fusion, f32[128]{0:T(128)} %divide_subtract_fusion, f32[3456]{0:T(1024)S(1)} %convert_element_type.40), kind=kOutput, calls=%fused_computation.7 | convolution fusion | flops 910016512 | bytes 10631168 | tf_op jit(solution)/shard_map/dot_general | solution.py:66
  112.5 2.1 slice.21
  114.6 2.9 %reshape.165 = bf16[3328,128]{1,0:T(8,128)(2,1)} reshape(bf16[128,3328]{1,0:T(8,128)(2,1)} %slice.21) | data formatting | bytes 1703936 | tf_op jit(solution)/shard_map/reshape | solution.py:71
  117.5 14.9 %scatter_custom_fusion.1 = bf16[4992,128]{1,0:T(8,128)(2,1)} fusion(s32[3328]{0:T(1024)} %copy-done.2, bf16[3328,128]{1,0:T(8,128)(2,1)} %reshape.165, bf16[]{:T(256)} %constant.5.clone.1), kind=kCustom, calls=%fused_computation.21 | custom fusion | bytes 1278464 | tf_op jit(solution)/shard_map/scatter | solution.py:73
  132.3 4.3 %all-to-all-start.2 = ((bf16[8,624,128]{2,1,0:T(8,128)(2,1)}), bf16[8,624,128]{2,1,0:T(8,128)(2,1)}, u32[]{:S(2)}, u32[]{:S(2)}) async-start(bf16[8,624,128]{2,1,0:T(8,128)(2,1)} %bitcast.33), calls=%async_computation.2 | async-start | bytes 2555904 | tf_op jit(solution)/shard_map/all_to_all | solution.py:75
  136.6 0.2 all-reduce.2.cloned.1.call-start
  136.8 1.4 reduce.5
  138.2 1.4 reshape.128
  139.6 1.4 fusion.21
  141.0 13.4 %all-to-all-done.2 = bf16[8,624,128]{2,1,0:T(8,128)(2,1)} async-done(((bf16[8,624,128]{2,1,0:T(8,128)(2,1)}), bf16[8,624,128]{2,1,0:T(8,128)(2,1)}, u32[]{:S(2)}, u32[]{:S(2)}) %all-to-all-start.2) | async-done | bytes 1277984 | tf_op jit(solution)/shard_map/all_to_all | solution.py:75
  154.5 33.9 %scatter_custom_fusion.2 = f32[2496,128]{1,0:T(8,128)} fusion(s32[4992]{0:T(1024)} %fusion.21, bf16[4992,128]{1,0:T(8,128)(2,1)} %bitcast.8, f32[]{:T(128)} %constant.9.clone.1), kind=kCustom, calls=%fused_computation.9 | custom fusion | flops 1277952 | bytes 2556416 | tf_op jit(solution)/shard_map/scatter-add | solution.py:85
  188.4 2.2 convert_element_type.47
  190.6 0.0 all-reduce.2.cloned.1.call-update
  190.6 1.4 slice.22
  192.0 1.5 fusion.3
  193.5 43.2 %all-gather.1 = f32[32,1,3456]{2,1,0:T(1,128)} all-gather(f32[1,1,3456]{2,1,0:T(1,128)S(1)} %reshape.179), channel_id=2, replica_groups=mesh['grp'=4,'emb'=8] {'grp','emb'}, dimensions={0}, use_global_device_ids=true | all-gather | bytes 456192 | tf_op jit(solution)/shard_map/all_gather | solution.py:90
  236.7 1.9 reduce_sum.52
  238.6 0.0 all-reduce.2.cloned.1.call-done
  238.6 2.3 reshape.135
  (2 shorter events, 0.0 us)
Async XLA Ops:
  7.2 92.5 %copy-start = (bf16[3456,512]{1,0:T(8,128)(2,1)S(1)}, bf16[3456,512]{1,0:T(8,128)(2,1)}, u32[]{:S(2)}) copy-start(bf16[3456,512]{1,0:T(8,128)(2,1)} %param.17) | copy-start | bytes 10616836
  22.2 41.2 %copy-start.2 = (s32[3328]{0:T(1024)}, s32[3328]{0:T(1024)S(1)}, u32[]{:S(2)}) copy-start(s32[3328]{0:T(1024)S(1)} %fusion.22) | copy-start | bytes 39940
  47.1 0.6 copy-start.1
  63.4 22.1 %all-to-all-start.1 = ((bf16[8,624,128]{2,1,0:T(8,128)(2,1)}), bf16[8,624,128]{2,1,0:T(8,128)(2,1)}, u32[]{:S(2)}, u32[]{:S(2)}) async-start(bf16[8,624,128]{2,1,0:T(8,128)(2,1)} %bitcast.34), calls=%async_computation.1 | async-start | bytes 2555904 | tf_op jit(solution)/shard_map/all_to_all | solution.py:41
  132.3 22.1 %all-to-all-start.2 = ((bf16[8,624,128]{2,1,0:T(8,128)(2,1)}), bf16[8,624,128]{2,1,0:T(8,128)(2,1)}, u32[]{:S(2)}, u32[]{:S(2)}) async-start(bf16[8,624,128]{2,1,0:T(8,128)(2,1)} %bitcast.33), calls=%async_computation.2 | async-start | bytes 2555904 | tf_op jit(solution)/shard_map/all_to_all | solution.py:75
  136.6 102.0 %all-reduce.2.cloned.1.call-start = ((), (), s32[]{:S(2)}) async-start(), calls=%async_computation.3 | async-start | bytes 1277952 | tf_op jit(solution)/shard_map/psum | solution.py:87
Sparse Core Ops, SparseCore 0:
  190.7 40.6 all-reduce.1
